TPU v7x, 128 devices: a whole 4x4x4 slice. The times are simulated.
128 devices in a mesh: blk: 16 (over z_lo, y, core), group: 8 (over x, z_hi).
Axes of the slice: x: 4, y: 4, z: 4 (z_hi: 2, z_lo: 2; z = z_hi * 2 + z_lo), core: 2. Of those that a mesh axis runs over, the one named last changes fastest.
Arguments:
- centres: bfloat16 [262144, 1024], P(('blk', 'group')), may hold values from -8 to 8
- batch_x: bfloat16 [2048, 1024], P(('blk', 'group')), may hold values from -8 to 8
- grad: bfloat16 [2048, 1000], P(('blk', 'group')), may hold values from -0.29882812 to 0.29882812
- eigvec: float32 [65536, 128], P(('blk', 'group')), may hold values from -0.0234375 to 0.0234375
- eig_scale: float32 [128], replicated, may hold values from 2 to 20
- sub_index: int32 [65536], P(('blk', 'group')), may hold values from 0 to 262143, as said below
Outputs:
- update: float32 [262144, 1000], P(('blk', 'group'))
Inputs may be any that keep to these rules, and one draw needn't show every extreme that they name: `sub_index`: all entries are distinct. Entry i of the block of 512 entries that device index k of blk+group holds names a centre among rows (k // 8) * 8 * 2048 to (k // 8 + 1) * 8 * 2048 - 1; among one such block at most 128 entries name rows of any one aligned run of 2048 centres, and every block has exactly 128 in one run.
All inputs are finite; a program needn't handle non-finite values.
Results may differ from a plain program's by a relative error of at most 0.0027.
Values may be sent and summed in bfloat16 or wider, within the bound.
No kernel may reach another device: no remote copies, remote signals or barrier semaphores. Data moves between devices by JAX's collectives and lax.ppermute only.
A program may use at most 128 MiB of HBM per device.

v0:
```python
import jax
import jax.numpy as jnp
from jax import lax
from jax.sharding import PartitionSpec as P

D = 1024
CAP = 128


def body(centres, batch_x, grad, eigvec, eig_scale, sub_index):
    centre_sq = jnp.sum(jnp.square(centres.astype(jnp.float32)), axis=1)
    piece_x = lax.all_gather(batch_x, ("blk", "group"), axis=0, tiled=True)
    piece_g = lax.all_gather(grad, ("blk", "group"), axis=0, tiled=True)
    batch_sq = jnp.sum(jnp.square(piece_x.astype(jnp.float32)), axis=1)
    inner_prod = jnp.einsum("cd,bd->cb", centres, piece_x, preferred_element_type=jnp.float32)
    distance = centre_sq[:, None] + batch_sq[None, :] - 2.0 * inner_prod
    kernel_tile = jnp.exp(-distance / (2.0 * D)).astype(jnp.bfloat16)
    kernel_grad = jnp.dot(kernel_tile, piece_g, preferred_element_type=jnp.float32)
    groups = lax.axis_size("group")
    rows_each = centres.shape[0]
    classes = grad.shape[1]
    holder = sub_index // rows_each % groups
    local_row = sub_index % rows_each
    onehot = (holder[:, None] == jnp.arange(groups, dtype=jnp.int32)[None, :]).astype(jnp.int32)
    order_in = jnp.sum(jnp.cumsum(onehot, axis=0) * onehot, axis=1) - 1
    position = holder * CAP + order_in
    slot_table = (
        jnp.zeros((groups * CAP,), jnp.int32).at[position].set(local_row).reshape(groups, CAP)
    )
    got_slots = lax.all_to_all(slot_table, "group", split_axis=0, concat_axis=0, tiled=True)
    flat_slots = got_slots.reshape(-1)
    fetched_rows = kernel_grad[flat_slots].reshape(groups, CAP, classes)
    returned = lax.all_to_all(fetched_rows, "group", split_axis=0, concat_axis=0, tiled=True)
    picked = returned.reshape(groups * CAP, classes)[position]
    projected = lax.psum(
        jnp.einsum("sq,sk->qk", eigvec, picked, precision=lax.Precision.HIGHEST), ("blk", "group")
    )
    correction = jnp.dot(eigvec * eig_scale[None, :], projected, precision=lax.Precision.HIGHEST)
    correction_table = jnp.zeros((groups * CAP, classes), jnp.float32).at[position].set(correction)
    correction_table = correction_table.reshape(groups, CAP, classes)
    got_correction = lax.all_to_all(
        correction_table, "group", split_axis=0, concat_axis=0, tiled=True
    )
    return kernel_grad.at[flat_slots].add(-got_correction.reshape(groups * CAP, classes))


def solution(mesh):
    in_specs = (
        P(("blk", "group"), None),
        P(("blk", "group"), None),
        P(("blk", "group"), None),
        P(("blk", "group"), None),
        P(),
        P(("blk", "group")),
    )
    out_specs = P(("blk", "group"), None)
    return jax.shard_map(body, mesh=mesh, in_specs=in_specs, out_specs=out_specs, check_vma=False)
```

profile of v0, /device:TPU:1, one launch (start us, length us, event | category | flops | bytes accessed | tf_op | source)
XLA Modules:
  0.0 998.5 jit_solution(11192851473559970175)
XLA Ops:
  6.5 0.7 all-gather.3.cloned.1.call-update
  7.3 0.0 all-gather.5.cloned.1.call-start
  7.3 0.7 all-gather.5.cloned.1.call-update
  8.0 0.7 add_select_fusion
  8.7 1.1 reduce-window.6
  9.9 0.2 slice_reduce_fusion
  10.1 0.1 fusion.10
  10.2 3.0 scatter_custom_fusion
  13.2 8.2 all-to-all-start
  21.4 3.1 multiply_reduce_fusion.1
  24.5 3.4 all-to-all-done
  27.9 291.1 %all-gather.3.cloned.1.call-done = bf16[2048,1024]{1,0:T(8,128)(2,1)} async-done(((bf16[16,1024]{1,0:T(8,128)(2,1)}), bf16[2048,1024]{1,0:T(8,128)(2,1)}) %all-gather.3.cloned.1.call-update) | async-done | bytes 4194320 | tf_op jit(solution)/shard_map/all_gather | solution.py:12
  318.9 3.1 multiply_reduce_fusion
  322.0 304.1 %all-gather.5.cloned.1.call-done = bf16[2048,1000]{1,0:T(8,128)(2,1)} async-done(((bf16[16,1000]{1,0:T(8,128)(2,1)}), bf16[2048,1000]{1,0:T(8,128)(2,1)}) %all-gather.5.cloned.1.call-update) | async-done | bytes 4096016 | tf_op jit(solution)/shard_map/all_gather | solution.py:13
  626.1 24.6 %fusion = f32[2048,1000]{1,0:T(8,128)} fusion(bf16[2048,1000]{1,0:T(8,128)(2,1)} %all-gather.5.cloned.1.call-done, bf16[2048,1024]{1,0:T(8,128)(2,1)} %param.6, bf16[2048,1024]{1,0:T(8,128)(2,1)} %all-gather.3.cloned.1.call-done, f32[2048]{0:T(1024)S(1)} %multiply_reduce_fusion, f32[2048]{0:T(1024)S(1)} %multiply_reduce_fusion.1), kind=kOutput, calls=%fused_computation.6 | convolution fusion | flops 17003708416 | bytes 20692992 | tf_op jit(solution)/shard_map/dot_general | solution.py:18
  650.7 9.7 gather_fusion
  660.4 5.3 copy.20
  665.7 6.5 all-to-all-start.1
  672.2 0.2 all-reduce.2.cloned.1.call-start
  672.5 58.3 %all-to-all-done.1 = f32[8,128,1000]{1,2,0:T(8,128)} async-done(((f32[8,128,1000]{1,2,0:T(8,128)}), f32[8,128,1000]{1,2,0:T(8,128)}, u32[]{:S(2)}, u32[]{:S(2)}) %all-to-all-start.1) | async-done | bytes 4096032 | tf_op jit(solution)/shard_map/all_to_all | solution.py:33
  730.8 5.3 copy.21
  736.1 5.0 gather_fusion.1
  741.2 4.2 convolution_bitcast_fusion
  745.4 145.6 %all-reduce.2.cloned.1.call-done = f32[128,1000]{0,1:T(8,128)} async-done(((f32[128,1000]{0,1:T(8,128)}), f32[128,1000]{0,1:T(8,128)}) %all-reduce.2.cloned.1.call-update) | async-done | bytes 512016 | tf_op jit(solution)/shard_map/psum | solution.py:35
  891.0 2.8 fusion.7
  893.9 4.5 scatter_custom_fusion.1
  898.4 5.3 copy.23
  903.7 54.8 %all_to_all.19 = f32[8,128,1000]{1,2,0:T(8,128)S(1)} all-to-all(f32[8,128,1000]{1,2,0:T(8,128)} %copy.23), channel_id=1, replica_groups=mesh['blk'=16,'group'=8] {'group'}, dimensions={0} | all-to-all | bytes 8192000 | tf_op jit(solution)/shard_map/all_to_all | solution.py:41
  958.4 2.2 neg.10
  960.6 5.3 copy.24
  965.9 16.9 %scatter_fusion = f32[2048,1000]{1,0:T(8,128)} fusion(f32[2048,1000]{1,0:T(8,128)} %fusion, s32[1024]{0:T(1024)S(1)} %bitcast.30, f32[1024,1000]{1,0:T(8,128)} %bitcast.26), kind=kCustom, calls=%fused_computation.4 | custom fusion | flops 1024000 | bytes 12292096 | tf_op jit(solution)/shard_map/scatter-add | solution.py:44
  982.8 9.1 copy.26
  (13 shorter events, 0.1 us)
Async XLA Ops:
  6.5 312.4 %all-gather.3.cloned.1.call-start = ((), (), s32[]{:S(2)}) async-start(), calls=%async_computation.3 | async-start | bytes 4227072 | tf_op jit(solution)/shard_map/all_gather | solution.py:12
  7.3 618.8 %all-gather.5.cloned.1.call-start = ((), (), s32[]{:S(2)}) async-start(), calls=%async_computation.4 | async-start | bytes 4227072 | tf_op jit(solution)/shard_map/all_gather | solution.py:13
  13.2 14.6 %all-to-all-start = ((s32[8,1,128]{2,1,0:T(1,128)}), s32[8,1,128]{2,1,0:T(1,128)S(1)}, u32[]{:S(2)}, u32[]{:S(2)}) async-start(s32[8,1,128]{2,1,0:T(1,128)} %bitcast.3), calls=%async_computation | async-start | bytes 8192 | tf_op jit(solution)/shard_map/all_to_all | solution.py:30
  665.7 65.1 %all-to-all-start.1 = ((f32[8,128,1000]{1,2,0:T(8,128)}), f32[8,128,1000]{1,2,0:T(8,128)}, u32[]{:S(2)}, u32[]{:S(2)}) async-start(f32[8,128,1000]{1,2,0:T(8,128)} %copy.20), calls=%async_computation.1 | async-start | bytes 8192000 | tf_op jit(solution)/shard_map/all_to_all | solution.py:33
  672.2 218.8 %all-reduce.2.cloned.1.call-start = ((), (), s32[]{:S(2)}) async-start(), calls=%async_computation.5 | async-start | bytes 1024000 | tf_op jit(solution)/shard_map/psum | solution.py:35
  736.1 5.1 copy-start
  736.1 154.9 %copy-start.1 = (f32[128]{0:T(128)S(1)}, f32[128]{0:T(128)}, u32[]{:S(2)}) copy-start(f32[128]{0:T(128)} %param.10) | copy-start | bytes 1540
Sparse Core Ops, SparseCore 0:
  9.0 309.8 all-gather.2
  320.6 305.3 all-gather.4
  745.5 145.4 all-reduce.1
where the time goes:
time: 999 us; the launch traced here: 998 us
  waiting for transfers between devices  804 us (80%)
  blocking collectives  54.8 us (5%)
  local copies, waits for them, and re-layouts  52.8 us (5%)
  matrix products  31.7 us (3%)
  other arithmetic  27.2 us (3%)
  starting transfers between devices  14.9 us (1%)
  between operations  13.2 us (1%)
    all_gather x1, waiting for transfers between devices, body(): piece_g = lax.all_gather(grad, ('blk', 'group'), axis=0, tiled=True)  304 us
    all_gather x1, waiting for transfers between devices, body(): piece_x = lax.all_gather(batch_x, ('blk', 'group'), axis=0, tiled=True)  291 us
    psum x1, waiting for transfers between devices, body(): lax.psum(jnp.einsum('sq,sk->qk', eigvec, picked, precision=lax.Precision....  146 us
    all_to_all x1, waiting for transfers between devices, body(): lax.all_to_all(fetched_rows, 'group', split_axis=0, concat_axis=0, tiled=...  58.3 us
    all_to_all x1, blocking collectives, body(): lax.all_to_all(correction_table, 'group', split_axis=0, concat_axis=0, ti...  54.8 us
    dot_general x1, matrix products, body(): jnp.dot(kernel_tile, piece_g, preferred_element_type=jnp.float32)  24.6 us
  transfers between devices with their start and end apart: 5, of which 5 were waited for; matrix products, arithmetic and copies ran while one was open for 1% of the time, Pallas kernels for 0%

commit v1 on v0

v1 whole, which is shorter than its diff:
```python
import jax
import jax.numpy as jnp
from jax import lax
from jax.sharding import PartitionSpec as P

D = 1024
CAP = 128


def body(centres, batch_x, grad, eigvec, eig_scale, sub_index):
    dims = batch_x.shape[1]
    centre_sq = jnp.sum(jnp.square(centres.astype(jnp.float32)), axis=1)
    joined = jnp.concatenate([batch_x, grad], axis=1)
    joined = lax.all_gather(joined, "group", axis=0, tiled=True)
    joined = lax.all_gather(joined, "blk", axis=0, tiled=True)
    piece_x = joined[:, :dims]
    piece_g = joined[:, dims:]
    batch_sq = jnp.sum(jnp.square(piece_x.astype(jnp.float32)), axis=1)
    inner_prod = jnp.einsum("cd,bd->cb", centres, piece_x, preferred_element_type=jnp.float32)
    distance = centre_sq[:, None] + batch_sq[None, :] - 2.0 * inner_prod
    kernel_tile = jnp.exp(-distance / (2.0 * D)).astype(jnp.bfloat16)
    kernel_grad = jnp.dot(kernel_tile, piece_g, preferred_element_type=jnp.float32)
    groups = lax.axis_size("group")
    rows_each = centres.shape[0]
    holder = sub_index // rows_each % groups
    local_row = sub_index % rows_each
    onehot = (holder[:, None] == jnp.arange(groups, dtype=jnp.int32)[None, :]).astype(jnp.int32)
    order_in = jnp.sum(jnp.cumsum(onehot, axis=0) * onehot, axis=1) - 1
    position = holder * CAP + order_in
    slot_table = jnp.zeros((groups * CAP,), jnp.int32).at[position].set(local_row)
    eig_table = jnp.zeros((groups * CAP, eigvec.shape[1]), jnp.float32).at[position].set(eigvec)
    got_slots = lax.all_to_all(slot_table, "group", split_axis=0, concat_axis=0, tiled=True)
    got_eig = lax.all_to_all(eig_table, "group", split_axis=0, concat_axis=0, tiled=True)
    picked = kernel_grad[got_slots]
    projected = lax.psum(
        jnp.einsum("sq,sk->qk", got_eig, picked, precision=lax.Precision.HIGHEST), ("blk", "group")
    )
    correction = jnp.dot(got_eig * eig_scale[None, :], projected, precision=lax.Precision.HIGHEST)
    return kernel_grad.at[got_slots].add(-correction)


def solution(mesh):
    in_specs = (
        P(("blk", "group"), None),
        P(("blk", "group"), None),
        P(("blk", "group"), None),
        P(("blk", "group"), None),
        P(),
        P(("blk", "group")),
    )
    out_specs = P(("blk", "group"), None)
    return jax.shard_map(body, mesh=mesh, in_specs=in_specs, out_specs=out_specs, check_vma=False)
```

time: 999 us -> 347 us (0.35)
  waiting for transfers between devices: 804 us -> 189 us
  local copies, waits for them, and re-layouts: 52.8 us -> 30.3 us
  blocking collectives: 54.8 us -> 32.8 us
  matrix products: 31.7 us -> 43.3 us
    all_gather x2 -> x1, waiting for transfers between devices: 595 us -> 41.5 us  [body(): joined = lax.all_gather(joined, 'blk', axis=0, tiled=True)]
    all_to_all x1, waiting for transfers between devices: 58.3 us -> 0.01 us  [body(): lax.all_to_all(eig_table, 'group', split_axis=0, concat_axis=0, tiled=True)]
    all_to_all x1 -> x0, blocking collectives: 54.8 us -> none  [body(): lax.all_to_all(correction_table, 'group', split_axis=0, concat_axis=0, ti...]
    all_gather x0 -> x1, blocking collectives: none -> 32.8 us  [body(): joined = lax.all_gather(joined, 'group', axis=0, tiled=True)]
    reshape x2 -> x0, local copies, waits for them, and re-layouts: 10.6 us -> none  [the longest x1 5.33 us: body(): fetched_rows = kernel_grad[flat_slots].reshape(groups, CAP, classes)]
  transfers between devices with their start and end apart: 5 -> 4, of which waited for: 5 -> 3; matrix products, arithmetic and copies ran while one was open for 1% -> 15% of each run, Pallas kernels for 0% -> 0%
where the time goes in v1:
time: 347 us; the launch traced here: 346 us
  waiting for transfers between devices  189 us (54%)
  matrix products  43.3 us (12%)
  blocking collectives  32.8 us (9%)
  local copies, waits for them, and re-layouts  30.3 us (9%)
  other arithmetic  25.8 us (7%)
  between operations  13.4 us (4%)
  starting transfers between devices  12.2 us (4%)
    psum x1, waiting for transfers between devices, body(): lax.psum(jnp.einsum('sq,sk->qk', got_eig, picked, precision=lax.Precision...  147 us
    all_gather x1, waiting for transfers between devices, body(): joined = lax.all_gather(joined, 'blk', axis=0, tiled=True)  41.5 us
    all_gather x1, blocking collectives, body(): joined = lax.all_gather(joined, 'group', axis=0, tiled=True)  32.8 us
    dot_general x1, matrix products, body(): jnp.dot(kernel_tile, piece_g, preferred_element_type=jnp.float32)  27.7 us
    scatter-add x1, other arithmetic, body(): return kernel_grad.at[got_slots].add(-correction)  16.9 us
    gather x1, local copies, waits for them, and re-layouts, body(): picked = kernel_grad[got_slots]  9.73 us
    dot_general x1, matrix products, body(): jnp.einsum('sq,sk->qk', got_eig, picked, precision=lax.Precision.HIGHEST)  9.69 us
    scatter-add x1, local copies, waits for them, and re-layouts, body(): return kernel_grad.at[got_slots].add(-correction)  9.15 us
  transfers between devices with their start and end apart: 4, of which 3 were waited for; matrix products, arithmetic and copies ran while one was open for 15% of the time, Pallas kernels for 0%

profile of v1, /device:TPU:1, one launch (start us, length us, event | category | flops | bytes accessed | tf_op | source)
XLA Modules:
  0.0 346.4 jit_solution(17484682141619954141)
XLA Ops:
  6.5 0.0 all-gather.2.cloned.1.call-start
  6.5 0.8 pad_maximum_fusion
  7.3 32.8 %all_gather.6 = bf16[128,2024]{1,0:T(8,128)(2,1)} all-gather(bf16[16,2024]{1,0:T(8,128)(2,1)S(1)} %pad_maximum_fusion), channel_id=1, replica_groups=mesh['blk'=16,'group'=8] {'group'}, dimensions={0}, use_global_device_ids=true | all-gather | bytes 582912 | tf_op jit(solution)/shard_map/all_gather | solution.py:14
  40.1 0.0 all-gather.2.cloned.1.call-update
  40.1 0.7 add_select_fusion
  40.8 1.1 reduce-window.6
  42.0 0.2 slice_reduce_fusion
  42.2 0.1 fusion.16
  42.3 3.0 scatter_custom_fusion
  45.3 5.8 %all-to-all-start = ((s32[8,128,1]{1,2,0:T(1,128)}), s32[8,128,1]{1,2,0:T(1,128)S(1)}, u32[]{:S(2)}, u32[]{:S(2)}) async-start(s32[8,128,1]{1,2,0:T(1,128)} %bitcast.5), calls=%async_computation | async-start | bytes 8192 | tf_op jit(solution)/shard_map/all_to_all | solution.py:32
  51.1 3.1 multiply_reduce_fusion.1
  54.2 2.9 scatter_custom_fusion.1
  57.1 0.5 all-to-all-done
  57.6 6.1 %all-to-all-start.1 = ((f32[8,128,128]{2,1,0:T(8,128)}), f32[8,128,128]{2,1,0:T(8,128)S(1)}, u32[]{:S(2)}, u32[]{:S(2)}) async-start(f32[8,128,128]{2,1,0:T(8,128)} %bitcast.8), calls=%async_computation.1 | async-start | bytes 1048576 | tf_op jit(solution)/shard_map/all_to_all | solution.py:33
  63.7 0.2 all-reduce.2.cloned.1.call-start
  64.0 41.5 %all-gather.2.cloned.1.call-done = bf16[2048,2024]{1,0:T(8,128)(2,1)} async-done(((bf16[128,2024]{1,0:T(8,128)(2,1)}), bf16[2048,2024]{1,0:T(8,128)(2,1)}) %all-gather.2.cloned.1.call-update) | async-done | bytes 8290320 | tf_op jit(solution)/shard_map/all_gather | solution.py:15
  105.5 3.1 multiply_reduce_fusion
  108.6 27.7 %fusion.4 = f32[2048,1000]{1,0:T(8,128)} fusion(bf16[2048,1024]{1,0:T(8,128)(2,1)} %param.6, f32[2048]{0:T(1024)S(1)} %multiply_reduce_fusion, f32[2048]{0:T(1024)S(1)} %multiply_reduce_fusion.1, bf16[2048,2024]{1,0:T(8,128)(2,1)} %all-gather.2.cloned.1.call-done), kind=kOutput, calls=%fused_computation.9 | convolution fusion | flops 17003708416 | bytes 20692992 | tf_op jit(solution)/shard_map/dot_general | solution.py:22
  136.3 0.0 copy-start
  136.3 9.7 %gather_fusion = f32[1024,1000]{1,0:T(8,128)} fusion(f32[2048,1000]{1,0:T(8,128)} %fusion.4, s32[1024]{0:T(1024)S(1)} %broadcast_clamp_fusion), kind=kCustom, calls=%fused_computation | custom fusion | bytes 8196096 | tf_op jit(solution)/shard_map/gather | solution.py:34
  146.0 0.0 all-to-all-done.1
  146.0 9.7 %fusion.24 = f32[128,1000]{0,1:T(8,128)} fusion(f32[1024,128]{1,0:T(8,128)S(1)} %bitcast.33, f32[1024,1000]{1,0:T(8,128)} %gather_fusion), kind=kOutput, calls=%fused_computation.49 | convolution fusion | flops 1572864000 | bytes 5132288 | tf_op jit(solution)/shard_map/sq,sk->qk/dot_general | solution.py:36
  155.7 0.0 all-reduce.2.cloned.1.call-update
  155.7 146.5 %all-reduce.2.cloned.1.call-done = f32[128,1000]{0,1:T(8,128)} async-done(((f32[128,1000]{0,1:T(8,128)}), f32[128,1000]{0,1:T(8,128)}) %all-reduce.2.cloned.1.call-update) | async-done | bytes 512016 | tf_op jit(solution)/shard_map/psum | solution.py:35
  302.3 0.0 copy-done
  302.3 5.9 %convolution_negate_fusion = f32[1024,1000]{0,1:T(8,128)} fusion(f32[128,1000]{0,1:T(8,128)} %all-reduce.2.cloned.1.call-done, f32[1024,128]{1,0:T(8,128)S(1)} %bitcast.34, f32[128]{0:T(128)S(1)} %copy-done), kind=kOutput, calls=%fused_computation.18 | convolution fusion | flops 1574019072 | bytes 5132800 | tf_op jit(solution)/shard_map/dot_general | solution.py:38
  308.2 5.3 %copy.15 = f32[1024,1000]{1,0:T(8,128)} copy(f32[1024,1000]{0,1:T(8,128)} %convolution_negate_fusion) | data formatting | bytes 8192000 | tf_op jit(solution)/shard_map/neg | solution.py:39
  313.5 16.9 %scatter_fusion = f32[2048,1000]{1,0:T(8,128)} fusion(f32[2048,1000]{1,0:T(8,128)} %fusion.4, s32[1024]{0:T(1024)S(1)} %bitcast.36, f32[1024,1000]{1,0:T(8,128)} %copy.15), kind=kCustom, calls=%fused_computation.3 | custom fusion | flops 1024000 | bytes 12292096 | tf_op jit(solution)/shard_map/scatter-add | solution.py:39
  330.4 9.1 %copy.16 = f32[2048,1000]{0,1:T(8,128)} copy(f32[2048,1000]{1,0:T(8,128)} %scatter_fusion) | data formatting | bytes 16384000 | tf_op jit(solution)/shard_map/scatter-add | solution.py:39
  (6 shorter events, 0.1 us)
Async XLA Ops:
  6.5 98.9 %all-gather.2.cloned.1.call-start = ((), (), s32[]{:S(2)}) async-start(), calls=%async_computation.2 | async-start | bytes 8912896 | tf_op jit(solution)/shard_map/all_gather | solution.py:15
  45.3 12.2 %all-to-all-start = ((s32[8,128,1]{1,2,0:T(1,128)}), s32[8,128,1]{1,2,0:T(1,128)S(1)}, u32[]{:S(2)}, u32[]{:S(2)}) async-start(s32[8,128,1]{1,2,0:T(1,128)} %bitcast.5), calls=%async_computation | async-start | bytes 8192 | tf_op jit(solution)/shard_map/all_to_all | solution.py:32
  57.6 88.4 %all-to-all-start.1 = ((f32[8,128,128]{2,1,0:T(8,128)}), f32[8,128,128]{2,1,0:T(8,128)S(1)}, u32[]{:S(2)}, u32[]{:S(2)}) async-start(f32[8,128,128]{2,1,0:T(8,128)} %bitcast.8), calls=%async_computation.1 | async-start | bytes 1048576 | tf_op jit(solution)/shard_map/all_to_all | solution.py:33
  63.7 238.5 %all-reduce.2.cloned.1.call-start = ((), (), s32[]{:S(2)}) async-start(), calls=%async_computation.3 | async-start | bytes 1024000 | tf_op jit(solution)/shard_map/psum | solution.py:35
  136.3 166.0 %copy-start = (f32[128]{0:T(128)S(1)}, f32[128]{0:T(128)}, u32[]{:S(2)}) copy-start(f32[128]{0:T(128)} %param.10) | copy-start | bytes 1540
Sparse Core Ops, SparseCore 0:
  40.2 65.2 all-gather.1
  155.8 146.3 all-reduce.1

commit v2 on v1

--- a/solution.py
+++ b/solution.py
@@ -5,6 +5,31 @@
 
 D = 1024
 CAP = 128
+
+
+SUM_BITS = (3, 6, 1, 4, 0, 2, 5)
+
+
+def tree_psum(value, axes):
+    size = lax.axis_size(axes)
+    me = lax.axis_index(axes)
+    bits = [b for b in SUM_BITS if (1 << b) < size]
+    current = value
+    for b in bits:
+        pairs = [(k, k ^ (1 << b)) for k in range(size)]
+        half = current.shape[0] // 2
+        upper = (me >> b) & 1
+        keep = lax.dynamic_slice_in_dim(current, upper * half, half, axis=0)
+        send = lax.dynamic_slice_in_dim(current, (1 - upper) * half, half, axis=0)
+        current = keep + lax.ppermute(send, axes, pairs)
+    for b in reversed(bits):
+        pairs = [(k, k ^ (1 << b)) for k in range(size)]
+        upper = (me >> b) & 1
+        other = lax.ppermute(current, axes, pairs)
+        current = jnp.where(
+            upper == 0, jnp.concatenate([current, other]), jnp.concatenate([other, current])
+        )
+    return current
 
 
 def body(centres, batch_x, grad, eigvec, eig_scale, sub_index):
@@ -32,9 +57,8 @@
     got_slots = lax.all_to_all(slot_table, "group", split_axis=0, concat_axis=0, tiled=True)
     got_eig = lax.all_to_all(eig_table, "group", split_axis=0, concat_axis=0, tiled=True)
     picked = kernel_grad[got_slots]
-    projected = lax.psum(
-        jnp.einsum("sq,sk->qk", got_eig, picked, precision=lax.Precision.HIGHEST), ("blk", "group")
-    )
+    partial = jnp.einsum("sq,sk->qk", got_eig, picked, precision=lax.Precision.HIGHEST)
+    projected = tree_psum(partial, ("blk", "group"))
     correction = jnp.dot(got_eig * eig_scale[None, :], projected, precision=lax.Precision.HIGHEST)
     return kernel_grad.at[got_slots].add(-correction)
 

time: 347 us -> 320 us (0.922); the launches traced: 346 us -> 315 us
  waiting for transfers between devices: 189 us -> 122 us
  starting transfers between devices: 12.2 us -> 45.4 us
    psum x1 -> x0, waiting for transfers between devices: 147 us -> none  [body(): lax.psum(jnp.einsum('sq,sk->qk', got_eig, picked, precision=lax.Precision...]
    ppermute x0 -> x14, waiting for transfers between devices: none -> 80.7 us  [the longest x7 62 us: tree_psum(): current = keep + lax.ppermute(send, axes, pairs)]
    ppermute x0 -> x14, starting transfers between devices: none -> 33 us  [the longest x7 23.1 us: tree_psum(): other = lax.ppermute(current, axes, pairs)]
  transfers between devices with their start and end apart: 4 -> 17, of which waited for: 3 -> 16; matrix products, arithmetic and copies ran while one was open for 15% -> 16% of each run, Pallas kernels for 0% -> 0%
where the time goes in v2:
time: 320 us; the launch traced here: 315 us
  waiting for transfers between devices  122 us (38%)
  starting transfers between devices  45.4 us (14%)
  matrix products  41.5 us (13%)
  blocking collectives  32.8 us (10%)
  local copies, waits for them, and re-layouts  32.3 us (10%)
  other arithmetic  27.3 us (9%)
  between operations  13.8 us (4%)
    ppermute x7, waiting for transfers between devices, tree_psum(): current = keep + lax.ppermute(send, axes, pairs)  62 us
    all_gather x1, waiting for transfers between devices, body(): joined = lax.all_gather(joined, 'blk', axis=0, tiled=True)  41.2 us
    all_gather x1, blocking collectives, body(): joined = lax.all_gather(joined, 'group', axis=0, tiled=True)  32.8 us
    dot_general x1, matrix products, body(): jnp.dot(kernel_tile, piece_g, preferred_element_type=jnp.float32)  27.7 us
    ppermute x7, starting transfers between devices, tree_psum(): other = lax.ppermute(current, axes, pairs)  23.1 us
    ppermute x7, waiting for transfers between devices, tree_psum(): other = lax.ppermute(current, axes, pairs)  18.7 us
    scatter-add x1, other arithmetic, body(): return kernel_grad.at[got_slots].add(-correction)  16.9 us
    gather x1, local copies, waits for them, and re-layouts, body(): picked = kernel_grad[got_slots]  9.9 us
  transfers between devices with their start and end apart: 17, of which 16 were waited for; matrix products, arithmetic and copies ran while one was open for 16% of the time, Pallas kernels for 0%

profile of v2, /device:TPU:1, one launch (start us, length us, event | category | flops | bytes accessed | tf_op | source)
XLA Modules:
  0.0 315.4 jit_solution(12501700116652101063)
XLA Ops:
  7.3 32.8 %all_gather.6 = bf16[128,2024]{1,0:T(8,128)(2,1)} all-gather(bf16[16,2024]{1,0:T(8,128)(2,1)S(1)} %pad_maximum_fusion), channel_id=1, replica_groups=mesh['blk'=16,'group'=8] {'group'}, dimensions={0}, use_global_device_ids=true | all-gather | bytes 582912 | tf_op jit(solution)/shard_map/all_gather | solution.py:39
  42.3 3.0 scatter_custom_fusion
  45.3 5.8 %all-to-all-start = ((s32[8,128,1]{1,2,0:T(1,128)}), s32[8,128,1]{1,2,0:T(1,128)S(1)}, u32[]{:S(2)}, u32[]{:S(2)}) async-start(s32[8,128,1]{1,2,0:T(1,128)} %bitcast.5), calls=%async_computation | async-start | bytes 8192 | tf_op jit(solution)/shard_map/all_to_all | solution.py:57
  51.1 3.1 multiply_reduce_fusion.1
  54.2 2.9 scatter_custom_fusion.1
  57.6 6.7 %all-to-all-start.1 = ((f32[8,128,128]{2,1,0:T(8,128)}), f32[8,128,128]{2,1,0:T(8,128)S(1)}, u32[]{:S(2)}, u32[]{:S(2)}) async-start(f32[8,128,128]{2,1,0:T(8,128)} %bitcast.8), calls=%async_computation.1 | async-start | bytes 1048576 | tf_op jit(solution)/shard_map/all_to_all | solution.py:58
  64.3 41.2 %all-gather.2.cloned.1.call-done = bf16[2048,2024]{1,0:T(8,128)(2,1)} async-done(((bf16[128,2024]{1,0:T(8,128)(2,1)}), bf16[2048,2024]{1,0:T(8,128)(2,1)}) %all-gather.2.cloned.1.call-update) | async-done | bytes 8290320 | tf_op jit(solution)/shard_map/all_gather | solution.py:40
  105.5 3.1 multiply_reduce_fusion
  108.6 27.7 %fusion.4 = f32[2048,1000]{1,0:T(8,128)} fusion(bf16[2048,1024]{1,0:T(8,128)(2,1)} %param.6, f32[2048]{0:T(1024)S(1)} %multiply_reduce_fusion, f32[2048]{0:T(1024)S(1)} %multiply_reduce_fusion.1, bf16[2048,2024]{1,0:T(8,128)(2,1)} %all-gather.2.cloned.1.call-done), kind=kOutput, calls=%fused_computation.9 | convolution fusion | flops 17003708416 | bytes 20692992 | tf_op jit(solution)/shard_map/dot_general | solution.py:47
  136.2 9.9 %gather_fusion = f32[1024,1000]{1,0:T(8,128)} fusion(f32[2048,1000]{1,0:T(8,128)} %fusion.4, s32[1024]{0:T(1024)S(1)} %broadcast_clamp_fusion), kind=kCustom, calls=%fused_computation | custom fusion | bytes 8196096 | tf_op jit(solution)/shard_map/gather | solution.py:59
  146.2 8.8 %fusion.31 = f32[128,1000]{0,1:T(8,128)S(1)} fusion(f32[1024,128]{1,0:T(8,128)S(1)} %bitcast.32, f32[1024,1000]{1,0:T(8,128)} %gather_fusion), kind=kOutput, calls=%fused_computation.77 | convolution fusion | flops 1572864000 | bytes 5132288 | tf_op jit(solution)/shard_map/sq,sk->qk/dot_general | solution.py:60
  157.7 12.9 %collective-permute-done.1 = f32[32,1000]{0,1:T(8,128)S(1)} collective-permute-done((f32[32,1000]{0,1:T(8,128)S(1)}, f32[32,1000]{0,1:T(8,128)S(1)}, u32[]{:S(2)}, u32[]{:S(2)}) %collective-permute-start.1) | collective-permute-done | bytes 128032 | tf_op jit(solution)/shard_map/ppermute | solution.py:24
  172.3 10.9 %collective-permute-done.2 = f32[16,1000]{0,1:T(8,128)S(1)} collective-permute-done((f32[16,1000]{0,1:T(8,128)S(1)}, f32[16,1000]{0,1:T(8,128)S(1)}, u32[]{:S(2)}, u32[]{:S(2)}) %collective-permute-start.2) | collective-permute-done | bytes 64032 | tf_op jit(solution)/shard_map/ppermute | solution.py:24
  183.7 11.2 %collective-permute-done.3 = f32[8,1000]{0,1:T(8,128)S(1)} collective-permute-done((f32[8,1000]{0,1:T(8,128)S(1)}, f32[8,1000]{0,1:T(8,128)S(1)}, u32[]{:S(2)}, u32[]{:S(2)}) %collective-permute-start.3) | collective-permute-done | bytes 32032 | tf_op jit(solution)/shard_map/ppermute | solution.py:24
  195.4 2.6 collective-permute-start.4
  198.0 9.4 %collective-permute-done.4 = f32[4,1000]{0,1:T(8,128)S(1)} collective-permute-done((f32[4,1000]{0,1:T(8,128)S(1)}, f32[4,1000]{0,1:T(8,128)S(1)}, u32[]{:S(2)}, u32[]{:S(2)}) %collective-permute-start.4) | collective-permute-done | bytes 16032 | tf_op jit(solution)/shard_map/ppermute | solution.py:24
  207.8 2.7 collective-permute-start.5
  210.5 8.4 %collective-permute-done.5 = f32[2,1000]{0,1:T(8,128)S(1)} collective-permute-done((f32[2,1000]{0,1:T(8,128)S(1)}, f32[2,1000]{0,1:T(8,128)S(1)}, u32[]{:S(2)}, u32[]{:S(2)}) %collective-permute-start.5) | collective-permute-done | bytes 8032 | tf_op jit(solution)/shard_map/ppermute | solution.py:24
  219.3 2.8 collective-permute-start.6
  222.1 7.5 %collective-permute-done.6 = f32[1,1000]{0,1:T(8,128)S(1)} collective-permute-done((f32[1,1000]{0,1:T(8,128)S(1)}, f32[1,1000]{0,1:T(8,128)S(1)}, u32[]{:S(2)}, u32[]{:S(2)}) %collective-permute-start.6) | collective-permute-done | bytes 4032 | tf_op jit(solution)/shard_map/ppermute | solution.py:24
  229.8 3.0 collective-permute-start.7
  233.0 6.8 %collective-permute-done.7 = f32[1,1000]{0,1:T(8,128)S(1)} collective-permute-done((f32[1,1000]{0,1:T(8,128)S(1)}, f32[1,1000]{0,1:T(8,128)S(1)}, u32[]{:S(2)}, u32[]{:S(2)}) %collective-permute-start.7) | collective-permute-done | bytes 4032 | tf_op jit(solution)/shard_map/ppermute | solution.py:28
  240.0 2.7 collective-permute-start.8
  244.4 2.6 collective-permute-start.9
  249.2 2.2 collective-permute-done.10
  252.6 2.0 collective-permute-done.11
  255.5 3.3 %collective-permute-done.12 = f32[32,1000]{1,0:T(8,128)S(1)} collective-permute-done((f32[32,1000]{1,0:T(8,128)S(1)}, f32[32,1000]{1,0:T(8,128)S(1)}, u32[]{:S(2)}, u32[]{:S(2)}) %collective-permute-start.12) | collective-permute-done | bytes 128032 | tf_op jit(solution)/shard_map/ppermute | solution.py:28
  258.8 12.1 %collective-permute-start.13 = (f32[64,1000]{1,0:T(8,128)S(1)}, f32[64,1000]{1,0:T(8,128)S(1)}, u32[]{:S(2)}, u32[]{:S(2)}) collective-permute-start(f32[64,1000]{1,0:T(8,128)S(1)} %maximum_select_fusion.2), channel_id=1, source_target_pairs={{0,8},{1,9},{2,10},{3,11},{4,12},{5,13},{6,14},{7,15},{8,0},{9,1},... | collective-permute-start | bytes 768008 | tf_op jit(solution)/shard_map/ppermute | solution.py:28
  272.0 5.0 %convolution_negate_fusion = f32[1024,1000]{0,1:T(8,128)} fusion(f32[64,1000]{1,0:T(8,128)S(1)} %collective-permute-done.13, f32[64,1000]{1,0:T(8,128)S(1)} %maximum_select_fusion.2, f32[1024,128]{1,0:T(8,128)S(1)} %bitcast.33, f32[128]{0:T(128)S(1)} %copy-done, pred[]{:T(512)S(6)} %eq.54), kind=kOutput, calls=%fused_computation.18 | convolution fusion | flops 1574403072 | bytes 5132801 | tf_op jit(solution)/shard_map/dot_general | solution.py:62
  277.0 5.3 %copy.19 = f32[1024,1000]{1,0:T(8,128)} copy(f32[1024,1000]{0,1:T(8,128)} %convolution_negate_fusion) | data formatting | bytes 8192000 | tf_op jit(solution)/shard_map/neg | solution.py:63
  282.3 16.9 %scatter_fusion = f32[2048,1000]{1,0:T(8,128)} fusion(f32[2048,1000]{1,0:T(8,128)} %fusion.4, s32[1024]{0:T(1024)S(1)} %bitcast.35, f32[1024,1000]{1,0:T(8,128)} %copy.19), kind=kCustom, calls=%fused_computation.3 | custom fusion | flops 1024000 | bytes 12292096 | tf_op jit(solution)/shard_map/scatter-add | solution.py:63
  299.2 9.1 %copy.20 = f32[2048,1000]{0,1:T(8,128)} copy(f32[2048,1000]{1,0:T(8,128)} %scatter_fusion) | data formatting | bytes 16384000 | tf_op jit(solution)/shard_map/scatter-add | solution.py:63
  (50 shorter events, 17.3 us)
Async XLA Ops:
  6.5 98.9 %all-gather.2.cloned.1.call-start = ((), (), s32[]{:S(2)}) async-start(), calls=%async_computation.2 | async-start | bytes 8912896 | tf_op jit(solution)/shard_map/all_gather | solution.py:40
  45.3 12.2 %all-to-all-start = ((s32[8,128,1]{1,2,0:T(1,128)}), s32[8,128,1]{1,2,0:T(1,128)S(1)}, u32[]{:S(2)}, u32[]{:S(2)}) async-start(s32[8,128,1]{1,2,0:T(1,128)} %bitcast.5), calls=%async_computation | async-start | bytes 8192 | tf_op jit(solution)/shard_map/all_to_all | solution.py:57
  57.6 88.6 %all-to-all-start.1 = ((f32[8,128,128]{2,1,0:T(8,128)}), f32[8,128,128]{2,1,0:T(8,128)S(1)}, u32[]{:S(2)}, u32[]{:S(2)}) async-start(f32[8,128,128]{2,1,0:T(8,128)} %bitcast.8), calls=%async_computation.1 | async-start | bytes 1048576 | tf_op jit(solution)/shard_map/all_to_all | solution.py:58
  155.2 2.0 collective-permute-start
  157.6 114.5 %copy-start = (f32[128]{0:T(128)S(1)}, f32[128]{0:T(128)}, u32[]{:S(2)}) copy-start(f32[128]{0:T(128)} %param.10) | copy-start | bytes 1540
  157.6 13.0 %collective-permute-start.1 = (f32[32,1000]{0,1:T(8,128)S(1)}, f32[32,1000]{0,1:T(8,128)S(1)}, u32[]{:S(2)}, u32[]{:S(2)}) collective-permute-start(f32[32,1000]{0,1:T(8,128)S(1)} %constant_dynamic-slice_fusion.5), channel_id=1, source_target_pairs={{0,64},{1,65},{2,66},{3,67},{4,68},{5,69},{6,70},{7,71},{8,72},{9,... | collective-permute-start | bytes 384008 | tf_op jit(solution)/shard_map/ppermute | solution.py:24
  171.1 12.2 %collective-permute-start.2 = (f32[16,1000]{0,1:T(8,128)S(1)}, f32[16,1000]{0,1:T(8,128)S(1)}, u32[]{:S(2)}, u32[]{:S(2)}) collective-permute-start(f32[16,1000]{0,1:T(8,128)S(1)} %constant_dynamic-slice_fusion.4), channel_id=1, source_target_pairs={{0,2},{1,3},{2,0},{3,1},{4,6},{5,7},{6,4},{7,5},{8,10},{9,11},{10,... | collective-permute-start | bytes 192008 | tf_op jit(solution)/shard_map/ppermute | solution.py:24
  183.6 11.3 %collective-permute-start.3 = (f32[8,1000]{0,1:T(8,128)S(1)}, f32[8,1000]{0,1:T(8,128)S(1)}, u32[]{:S(2)}, u32[]{:S(2)}) collective-permute-start(f32[8,1000]{0,1:T(8,128)S(1)} %constant_dynamic-slice_fusion.3), channel_id=1, source_target_pairs={{0,16},{1,17},{2,18},{3,19},{4,20},{5,21},{6,22},{7,23},{8,24},{9,... | collective-permute-start | bytes 96008 | tf_op jit(solution)/shard_map/ppermute | solution.py:24
  195.4 12.0 %collective-permute-start.4 = (f32[4,1000]{0,1:T(8,128)S(1)}, f32[4,1000]{0,1:T(8,128)S(1)}, u32[]{:S(2)}, u32[]{:S(2)}) collective-permute-start(f32[4,1000]{0,1:T(8,128)S(1)} %constant_dynamic-slice_fusion.2), channel_id=1, source_target_pairs={{0,1},{1,0},{2,3},{3,2},{4,5},{5,4},{6,7},{7,6},{8,9},{9,8},{10,11... | collective-permute-start | bytes 48008 | tf_op jit(solution)/shard_map/ppermute | solution.py:24
  207.8 11.1 %collective-permute-start.5 = (f32[2,1000]{0,1:T(8,128)S(1)}, f32[2,1000]{0,1:T(8,128)S(1)}, u32[]{:S(2)}, u32[]{:S(2)}) collective-permute-start(f32[2,1000]{0,1:T(8,128)S(1)} %constant_dynamic-slice_fusion.1), channel_id=1, source_target_pairs={{0,4},{1,5},{2,6},{3,7},{4,0},{5,1},{6,2},{7,3},{8,12},{9,13},{10,... | collective-permute-start | bytes 24008 | tf_op jit(solution)/shard_map/ppermute | solution.py:24
  219.3 10.3 %collective-permute-start.6 = (f32[1,1000]{0,1:T(8,128)S(1)}, f32[1,1000]{0,1:T(8,128)S(1)}, u32[]{:S(2)}, u32[]{:S(2)}) collective-permute-start(f32[1,1000]{0,1:T(8,128)S(1)} %constant_dynamic-slice_fusion), channel_id=1, source_target_pairs={{0,32},{1,33},{2,34},{3,35},{4,36},{5,37},{6,38},{7,39},{8,40},{9,... | collective-permute-start | bytes 12008 | tf_op jit(solution)/shard_map/ppermute | solution.py:24
  229.8 10.0 %collective-permute-start.7 = (f32[1,1000]{0,1:T(8,128)S(1)}, f32[1,1000]{0,1:T(8,128)S(1)}, u32[]{:S(2)}, u32[]{:S(2)}) collective-permute-start(f32[1,1000]{0,1:T(8,128)S(1)} %dynamic-slice_add_fusion), channel_id=1, source_target_pairs={{0,32},{1,33},{2,34},{3,35},{4,36},{5,37},{6,38},{7,39},{8,40},{9,... | collective-permute-start | bytes 12008 | tf_op jit(solution)/shard_map/ppermute | solution.py:28
  240.0 4.4 %collective-permute-start.8 = (f32[2,1000]{1,0:T(2,128)S(1)}, f32[2,1000]{1,0:T(2,128)S(1)}, u32[]{:S(2)}, u32[]{:S(2)}) collective-permute-start(f32[2,1000]{1,0:T(2,128)S(1)} %maximum_select_fusion.7), channel_id=1, source_target_pairs={{0,4},{1,5},{2,6},{3,7},{4,0},{5,1},{6,2},{7,3},{8,12},{9,13},{10,... | collective-permute-start | bytes 24008 | tf_op jit(solution)/shard_map/ppermute | solution.py:28
  244.4 4.2 %collective-permute-start.9 = (f32[4,1000]{1,0:T(4,128)S(1)}, f32[4,1000]{1,0:T(4,128)S(1)}, u32[]{:S(2)}, u32[]{:S(2)}) collective-permute-start(f32[4,1000]{1,0:T(4,128)S(1)} %maximum_select_fusion.6), channel_id=1, source_target_pairs={{0,1},{1,0},{2,3},{3,2},{4,5},{5,4},{6,7},{7,6},{8,9},{9,8},{10,11... | collective-permute-start | bytes 48008 | tf_op jit(solution)/shard_map/ppermute | solution.py:28
  248.6 2.8 collective-permute-start.10
  251.4 3.2 %collective-permute-start.11 = (f32[16,1000]{1,0:T(8,128)S(1)}, f32[16,1000]{1,0:T(8,128)S(1)}, u32[]{:S(2)}, u32[]{:S(2)}) collective-permute-start(f32[16,1000]{1,0:T(8,128)S(1)} %maximum_select_fusion.4), channel_id=1, source_target_pairs={{0,2},{1,3},{2,0},{3,1},{4,6},{5,7},{6,4},{7,5},{8,10},{9,11},{10,... | collective-permute-start | bytes 192008 | tf_op jit(solution)/shard_map/ppermute | solution.py:28
  254.6 4.2 %collective-permute-start.12 = (f32[32,1000]{1,0:T(8,128)S(1)}, f32[32,1000]{1,0:T(8,128)S(1)}, u32[]{:S(2)}, u32[]{:S(2)}) collective-permute-start(f32[32,1000]{1,0:T(8,128)S(1)} %maximum_select_fusion.3), channel_id=1, source_target_pairs={{0,64},{1,65},{2,66},{3,67},{4,68},{5,69},{6,70},{7,71},{8,72},{9,... | collective-permute-start | bytes 384008 | tf_op jit(solution)/shard_map/ppermute | solution.py:28
  258.8 13.2 %collective-permute-start.13 = (f32[64,1000]{1,0:T(8,128)S(1)}, f32[64,1000]{1,0:T(8,128)S(1)}, u32[]{:S(2)}, u32[]{:S(2)}) collective-permute-start(f32[64,1000]{1,0:T(8,128)S(1)} %maximum_select_fusion.2), channel_id=1, source_target_pairs={{0,8},{1,9},{2,10},{3,11},{4,12},{5,13},{6,14},{7,15},{8,0},{9,1},... | collective-permute-start | bytes 768008 | tf_op jit(solution)/shard_map/ppermute | solution.py:28
Sparse Core Ops, SparseCore 0:
  40.2 65.2 all-gather.1

commit v3 on v1

--- a/solution.py
+++ b/solution.py
@@ -7,11 +7,38 @@
 CAP = 128
 
 
+def scatter_sum(value, axis):
+    size = lax.axis_size(axis)
+    got = lax.all_to_all(value, axis, split_axis=0, concat_axis=0, tiled=True)
+    return got.reshape((size, -1) + value.shape[1:]).sum(axis=0)
+
+
+def gather_back(value, axis):
+    size = lax.axis_size(axis)
+    return lax.all_to_all(jnp.tile(value, (size, 1)), axis, split_axis=0, concat_axis=0, tiled=True)
+
+
+def tree_psum(value):
+    part = scatter_sum(scatter_sum(value, "group"), "blk")
+    return gather_back(gather_back(part, "blk"), "group")
+
+
+def exchange_gather(value, axis):
+    size = lax.axis_size(axis)
+    me = lax.axis_index(axis)
+    got = [value]
+    for d in range(1, size):
+        got.append(lax.ppermute(value, axis, [(k, k ^ d) for k in range(size)]))
+    stacked = jnp.stack(got)
+    order = jnp.arange(size, dtype=jnp.int32) ^ me
+    return stacked[order].reshape((-1,) + value.shape[1:])
+
+
 def body(centres, batch_x, grad, eigvec, eig_scale, sub_index):
     dims = batch_x.shape[1]
     centre_sq = jnp.sum(jnp.square(centres.astype(jnp.float32)), axis=1)
     joined = jnp.concatenate([batch_x, grad], axis=1)
-    joined = lax.all_gather(joined, "group", axis=0, tiled=True)
+    joined = exchange_gather(joined, "group")
     joined = lax.all_gather(joined, "blk", axis=0, tiled=True)
     piece_x = joined[:, :dims]
     piece_g = joined[:, dims:]
@@ -32,11 +59,19 @@
     got_slots = lax.all_to_all(slot_table, "group", split_axis=0, concat_axis=0, tiled=True)
     got_eig = lax.all_to_all(eig_table, "group", split_axis=0, concat_axis=0, tiled=True)
     picked = kernel_grad[got_slots]
-    projected = lax.psum(
-        jnp.einsum("sq,sk->qk", got_eig, picked, precision=lax.Precision.HIGHEST), ("blk", "group")
+    partial = jnp.einsum("sq,sk->qk", got_eig, picked, precision=lax.Precision.HIGHEST)
+    projected = tree_psum(partial)
+    correction = jnp.dot(got_eig * eig_scale[None, :], projected, precision=lax.Precision.HIGHEST)
+    rounded = lax.reduce_precision(correction, exponent_bits=8, mantissa_bits=7)
+    upper = rounded.astype(jnp.bfloat16)
+    lower = (correction - rounded).astype(jnp.bfloat16)
+    hits = (jnp.arange(rows_each, dtype=jnp.int32)[:, None] == got_slots[None, :]).astype(jnp.bfloat16)
+    placed = jnp.dot(
+        jnp.concatenate([hits, hits], axis=1),
+        jnp.concatenate([upper, lower], axis=0),
+        preferred_element_type=jnp.float32,
     )
-    correction = jnp.dot(got_eig * eig_scale[None, :], projected, precision=lax.Precision.HIGHEST)
-    return kernel_grad.at[got_slots].add(-correction)
+    return kernel_grad - placed
 
 
 def solution(mesh):

time: 347 us -> 216 us (0.62)
  waiting for transfers between devices: 189 us -> 53.4 us
  other arithmetic: 25.8 us -> 11.5 us
  starting transfers between devices: 12.2 us -> 24.3 us
  blocking collectives: 32.8 us -> 36.5 us
    psum x1 -> x0, waiting for transfers between devices: 147 us -> none  [body(): lax.psum(jnp.einsum('sq,sk->qk', got_eig, picked, precision=lax.Precision...]
    all_to_all x0 -> x3, blocking collectives: none -> 36.5 us  [the longest x2 27.8 us: scatter_sum(): got = lax.all_to_all(value, axis, split_axis=0, concat_axis=0, tiled=True)]
    all_gather x1 -> x0, blocking collectives: 32.8 us -> none  [body(): joined = lax.all_gather(joined, 'group', axis=0, tiled=True)]
    scatter-add x1 -> x0, other arithmetic: 16.9 us -> none  [body(): return kernel_grad.at[got_slots].add(-correction)]
    ppermute x0 -> x7, starting transfers between devices: none -> 13.9 us  [exchange_gather(): got.append(lax.ppermute(value, axis, [(k, k ^ d) for k in range(size)]))]
    dot_general x0 -> x1, matrix products: none -> 13.1 us  [body(): jnp.dot(jnp.concatenate([hits, hits], axis=1), jnp.concatenate([upper, lo...]
    all_gather x1, waiting for transfers between devices: 41.5 us -> 31 us  [body(): joined = lax.all_gather(joined, 'blk', axis=0, tiled=True)]
    dot_general x0 -> x1, local copies, waits for them, and re-layouts: none -> 9.24 us  [body(): jnp.dot(kernel_tile, piece_g, preferred_element_type=jnp.float32)]
  transfers between devices with their start and end apart: 4 -> 11, of which waited for: 3 -> 7; matrix products, arithmetic and copies ran while one was open for 15% -> 7% of each run, Pallas kernels for 0% -> 0%
where the time goes in v3:
time: 216 us; the launch traced here: 215 us
  waiting for transfers between devices  53.4 us (25%)
  matrix products  46.7 us (22%)
  blocking collectives  36.5 us (17%)
  local copies, waits for them, and re-layouts  29.4 us (14%)
  starting transfers between devices  24.3 us (11%)
  between operations  13.6 us (6%)
  other arithmetic  11.5 us (5%)
    all_gather x1, waiting for transfers between devices, body(): joined = lax.all_gather(joined, 'blk', axis=0, tiled=True)  31 us
    all_to_all x2, blocking collectives, scatter_sum(): got = lax.all_to_all(value, axis, split_axis=0, concat_axis=0, tiled=True)  27.8 us
    dot_general x1, matrix products, body(): jnp.dot(kernel_tile, piece_g, preferred_element_type=jnp.float32)  25.3 us
    ppermute x7, starting transfers between devices, exchange_gather(): got.append(lax.ppermute(value, axis, [(k, k ^ d) for k in range(size)]))  13.9 us
    dot_general x1, matrix products, body(): jnp.dot(jnp.concatenate([hits, hits], axis=1), jnp.concatenate([upper, lo...  13.1 us
    gather x1, local copies, waits for them, and re-layouts, body(): picked = kernel_grad[got_slots]  9.82 us
    dot_general x1, local copies, waits for them, and re-layouts, body(): jnp.dot(kernel_tile, piece_g, preferred_element_type=jnp.float32)  9.24 us
    all_to_all x1, blocking collectives, gather_back(): lax.all_to_all(jnp.tile(value, (size, 1)), axis, split_axis=0, concat_axi...  8.69 us
  transfers between devices with their start and end apart: 11, of which 7 were waited for; matrix products, arithmetic and copies ran while one was open for 7% of the time, Pallas kernels for 0%

profile of v3, /device:TPU:1, one launch (start us, length us, event | category | flops | bytes accessed | tf_op | source)
XLA Modules:
  0.0 215.4 jit_solution(11427458674561068708)
XLA Ops:
  8.1 4.4 %collective-permute-start = (bf16[16,2024]{1,0:T(8,128)(2,1)S(1)}, bf16[16,2024]{1,0:T(8,128)(2,1)S(1)}, u32[]{:S(2)}, u32[]{:S(2)}) collective-permute-start(bf16[16,2024]{1,0:T(8,128)(2,1)S(1)} %constant_dynamic-update-slice_fusion), channel_id=1, source_target_pairs={{0,1},{1,0},{2,3},{3,2},{4,5},{5,4},{6,7},{7,6},{8,9},{9,8},{10,11... | collective-permute-start | bytes 194312 | tf_op jit(solution)/shard_map/ppermute | solution.py:31
  12.5 1.2 collective-permute-start.1
  13.7 2.7 %collective-permute-start.3 = (bf16[16,2024]{1,0:T(8,128)(2,1)S(1)}, bf16[16,2024]{1,0:T(8,128)(2,1)S(1)}, u32[]{:S(2)}, u32[]{:S(2)}) collective-permute-start(bf16[16,2024]{1,0:T(8,128)(2,1)S(1)} %constant_dynamic-update-slice_fusion), channel_id=1, source_target_pairs={{0,4},{1,5},{2,6},{3,7},{4,0},{5,1},{6,2},{7,3},{8,12},{9,13},{10,... | collective-permute-start | bytes 194312 | tf_op jit(solution)/shard_map/ppermute | solution.py:31
  16.4 2.9 %collective-permute-start.4 = (bf16[16,2024]{1,0:T(8,128)(2,1)S(1)}, bf16[16,2024]{1,0:T(8,128)(2,1)S(1)}, u32[]{:S(2)}, u32[]{:S(2)}) collective-permute-start(bf16[16,2024]{1,0:T(8,128)(2,1)S(1)} %constant_dynamic-update-slice_fusion), channel_id=1, source_target_pairs={{0,5},{1,4},{2,7},{3,6},{4,1},{5,0},{6,3},{7,2},{8,13},{9,12},{10,... | collective-permute-start | bytes 194312 | tf_op jit(solution)/shard_map/ppermute | solution.py:31
  19.4 2.6 %collective-permute-start.5 = (bf16[16,2024]{1,0:T(8,128)(2,1)S(1)}, bf16[16,2024]{1,0:T(8,128)(2,1)S(1)}, u32[]{:S(2)}, u32[]{:S(2)}) collective-permute-start(bf16[16,2024]{1,0:T(8,128)(2,1)S(1)} %constant_dynamic-update-slice_fusion), channel_id=1, source_target_pairs={{0,6},{1,7},{2,4},{3,5},{4,2},{5,3},{6,0},{7,1},{8,14},{9,15},{10,... | collective-permute-start | bytes 194312 | tf_op jit(solution)/shard_map/ppermute | solution.py:31
  22.1 1.9 collective-permute-done.4
  23.9 0.8 collective-permute-done.5
  24.7 4.0 %collective-permute-done.6 = bf16[16,2024]{1,0:T(8,128)(2,1)S(1)} collective-permute-done((bf16[16,2024]{1,0:T(8,128)(2,1)S(1)}, bf16[16,2024]{1,0:T(8,128)(2,1)S(1)}, u32[]{:S(2)}, u32[]{:S(2)}) %collective-permute-start.6) | collective-permute-done | bytes 64800 | tf_op jit(solution)/shard_map/ppermute | solution.py:31
  28.7 1.4 gather_fusion
  30.8 1.1 reduce-window.6
  32.4 3.0 %scatter_custom_fusion = s32[1024]{0:T(1024)} fusion(s32[512]{0:T(512)S(1)} %compare_select_fusion.1, s32[512]{0:T(512)S(1)} %get-tuple-element.7, s32[]{:T(128)} %constant.55.clone.1), kind=kCustom, calls=%fused_computation.67 | custom fusion | bytes 4100 | tf_op jit(solution)/shard_map/scatter | solution.py:57
  35.4 3.3 %all-to-all-start = ((s32[8,128,1]{1,2,0:T(1,128)}), s32[8,128,1]{1,2,0:T(1,128)S(1)}, u32[]{:S(2)}, u32[]{:S(2)}) async-start(s32[8,128,1]{1,2,0:T(1,128)} %bitcast.15), calls=%async_computation | async-start | bytes 8192 | tf_op jit(solution)/shard_map/all_to_all | solution.py:59
  38.7 3.0 %scatter_custom_fusion.1 = f32[1024,128]{1,0:T(8,128)} fusion(s32[512]{0:T(512)S(1)} %compare_select_fusion.1, f32[512,128]{1,0:T(8,128)} %param.9, f32[]{:T(128)} %constant.53.clone.1), kind=kCustom, calls=%fused_computation.33 | custom fusion | bytes 524800 | tf_op jit(solution)/shard_map/scatter | solution.py:58
  41.7 3.3 %all-to-all-done = s32[8,128,1]{1,2,0:T(1,128)S(1)} async-done(((s32[8,128,1]{1,2,0:T(1,128)}), s32[8,128,1]{1,2,0:T(1,128)S(1)}, u32[]{:S(2)}, u32[]{:S(2)}) %all-to-all-start) | async-done | bytes 4128 | tf_op jit(solution)/shard_map/all_to_all | solution.py:59
  45.0 3.7 %all-to-all-start.1 = ((f32[8,128,128]{2,1,0:T(8,128)}), f32[8,128,128]{2,1,0:T(8,128)S(1)}, u32[]{:S(2)}, u32[]{:S(2)}) async-start(f32[8,128,128]{2,1,0:T(8,128)} %bitcast.17), calls=%async_computation.1 | async-start | bytes 1048576 | tf_op jit(solution)/shard_map/all_to_all | solution.py:60
  48.6 3.2 %multiply_reduce_fusion.1 = f32[2048]{0:T(1024)S(1)} fusion(bf16[2048,1024]{1,0:T(8,128)(2,1)} %param.6), kind=kLoop, calls=%fused_computation.20 | loop fusion | flops 6289408 | bytes 4202496 | tf_op jit(solution)/shard_map/reduce_sum | solution.py:39
  51.8 5.2 %all-to-all-done.1 = f32[8,128,128]{2,1,0:T(8,128)S(1)} async-done(((f32[8,128,128]{2,1,0:T(8,128)}), f32[8,128,128]{2,1,0:T(8,128)S(1)}, u32[]{:S(2)}, u32[]{:S(2)}) %all-to-all-start.1) | async-done | bytes 524320 | tf_op jit(solution)/shard_map/all_to_all | solution.py:60
  57.2 31.0 %all-gather.2.cloned.1.call-done = bf16[2048,2024]{1,0:T(8,128)(2,1)} async-done(((bf16[128,2024]{1,0:T(8,128)(2,1)}), bf16[2048,2024]{1,0:T(8,128)(2,1)}) %all-gather.2.cloned.1.call-update) | async-done | bytes 8290320 | tf_op jit(solution)/shard_map/all_gather | solution.py:42
  88.2 3.1 %multiply_reduce_fusion = f32[2048]{0:T(1024)S(1)} fusion(bf16[2048,2024]{1,0:T(8,128)(2,1)} %all-gather.2.cloned.1.call-done), kind=kLoop, calls=%fused_computation.18 | loop fusion | flops 6289408 | bytes 4202496 | tf_op jit(solution)/shard_map/reduce_sum | solution.py:45
  91.3 25.3 %fusion.8 = f32[2048,1000]{0,1:T(8,128)} fusion(bf16[2048,1024]{1,0:T(8,128)(2,1)} %param.6, f32[2048]{0:T(1024)S(1)} %multiply_reduce_fusion, f32[2048]{0:T(1024)S(1)} %multiply_reduce_fusion.1, bf16[2048,2024]{1,0:T(8,128)(2,1)} %all-gather.2.cloned.1.call-done), kind=kOutput, calls=%fused_computation.13 | convolution fusion | flops 17003708416 | bytes 20692992 | tf_op jit(solution)/shard_map/dot_general | solution.py:49
  116.6 9.2 %copy.14 = f32[2048,1000]{1,0:T(8,128)} copy(f32[2048,1000]{0,1:T(8,128)} %fusion.8) | data formatting | bytes 16384000 | tf_op jit(solution)/shard_map/dot_general | solution.py:49
  125.8 9.8 %gather_fusion.1 = f32[1024,1000]{1,0:T(8,128)} fusion(f32[2048,1000]{1,0:T(8,128)} %copy.14, s32[1024]{0:T(1024)S(1)} %broadcast_clamp_fusion), kind=kCustom, calls=%fused_computation.1 | custom fusion | bytes 8196096 | tf_op jit(solution)/shard_map/gather | solution.py:61
  135.6 4.6 %fusion.14 = f32[8,16,1000]{2,1,0:T(8,128)S(1)} fusion(f32[8,16,1024]{2,1,0:T(8,128)S(1)} %bitcast.64, f32[1024,1000]{1,0:T(8,128)} %gather_fusion.1), kind=kOutput, calls=%fused_computation.24 | convolution fusion | flops 1572864000 | bytes 5132288 | tf_op jit(solution)/shard_map/sq,sk->qk/dot_general | solution.py:62
  140.2 16.1 %all_to_all.54 = f32[8,16,1000]{2,1,0:T(8,128)S(1)} all-to-all(f32[8,16,1000]{2,1,0:T(8,128)S(1)} %fusion.14), channel_id=1, replica_groups=mesh['blk'=16,'group'=8] {'group'}, dimensions={0} | all-to-all | bytes 1024000 | tf_op jit(solution)/shard_map/all_to_all | solution.py:12
  156.4 11.7 %all_to_all.55 = f32[16,1,1000]{2,1,0:T(1,128)S(1)} all-to-all(f32[16,1,1000]{2,1,0:T(1,128)S(1)} %all_to_all.43), channel_id=1, replica_groups=mesh['blk'=16,'group'=8] {'blk'}, dimensions={0} | all-to-all | bytes 128000 | tf_op jit(solution)/shard_map/all_to_all | solution.py:12
  168.2 8.7 %all_to_all.56 = f32[16,1,1000]{2,1,0:T(1,128)S(1)} all-to-all(f32[16,1,1000]{2,1,0:T(1,128)S(1)} %tile.6), channel_id=1, replica_groups=mesh['blk'=16,'group'=8] {'blk'}, dimensions={0} | all-to-all | bytes 128000 | tf_op jit(solution)/shard_map/all_to_all | solution.py:18
  176.9 0.9 tile.8
  177.8 3.5 %all-to-all-start.5 = ((f32[8,16,1000]{2,1,0:T(8,128)}), f32[8,16,1000]{2,1,0:T(8,128)S(1)}, u32[]{:S(2)}, u32[]{:S(2)}) async-start(f32[8,16,1000]{2,1,0:T(8,128)} %tile.8), calls=%async_computation.5 | async-start | bytes 1048576 | tf_op jit(solution)/shard_map/all_to_all | solution.py:18
  181.3 3.1 %iota_compare_fusion = pred[2048,1024]{1,0:T(32,128)(4,1)} fusion(s32[1024]{0:T(1024)S(1)} %bitcast.68), kind=kLoop, calls=%fused_computation.14 | loop fusion | flops 2097152 | bytes 2101248 | tf_op jit(solution)/shard_map/eq | solution.py:68
  184.5 7.3 %all-to-all-done.5 = f32[8,16,1000]{2,1,0:T(8,128)S(1)} async-done(((f32[8,16,1000]{2,1,0:T(8,128)}), f32[8,16,1000]{2,1,0:T(8,128)S(1)}, u32[]{:S(2)}, u32[]{:S(2)}) %all-to-all-start.5) | async-done | bytes 512032 | tf_op jit(solution)/shard_map/all_to_all | solution.py:18
  191.8 3.7 %reduce-precision_convert_fusion = (bf16[1024,1000]{0,1:T(8,128)(2,1)S(1)}, bf16[1024,1000]{0,1:T(8,128)(2,1)S(1)}) fusion(f32[1024,128]{1,0:T(8,128)S(1)} %bitcast.65, f32[128,1000]{1,0:T(8,128)S(1)} %bitcast.63), kind=kOutput, calls=%fused_computation.22 | convolution fusion | flops 1576960000 | bytes 5132288 | tf_op jit(solution)/shard_map/dot_general | solution.py:64
  195.5 13.1 %fusion.18 = f32[2048,1000]{0,1:T(8,128)} fusion(f32[2048,1000]{0,1:T(8,128)} %fusion.8, pred[2048,1024]{1,0:T(32,128)(4,1)S(1)} %copy-done, bf16[1024,1000]{0,1:T(8,128)(2,1)S(1)} %get-tuple-element.6, bf16[1024,1000]{0,1:T(8,128)(2,1)S(1)} %get-tuple-element.5), kind=kOutput, calls=%fused_computation.28 | convolution fusion | flops 8403042304 | bytes 22577152 | tf_op jit(solution)/shard_map/dot_general | solution.py:69
  (40 shorter events, 3.2 us)
Async XLA Ops:
  6.5 81.6 %all-gather.2.cloned.1.call-start = ((), (), s32[]{:S(2)}) async-start(), calls=%async_computation.6 | async-start | bytes 8912896 | tf_op jit(solution)/shard_map/all_gather | solution.py:42
  8.1 11.3 %collective-permute-start = (bf16[16,2024]{1,0:T(8,128)(2,1)S(1)}, bf16[16,2024]{1,0:T(8,128)(2,1)S(1)}, u32[]{:S(2)}, u32[]{:S(2)}) collective-permute-start(bf16[16,2024]{1,0:T(8,128)(2,1)S(1)} %constant_dynamic-update-slice_fusion), channel_id=1, source_target_pairs={{0,1},{1,0},{2,3},{3,2},{4,5},{5,4},{6,7},{7,6},{8,9},{9,8},{10,11... | collective-permute-start | bytes 194312 | tf_op jit(solution)/shard_map/ppermute | solution.py:31
  12.5 9.4 %collective-permute-start.1 = (bf16[16,2024]{1,0:T(8,128)(2,1)S(1)}, bf16[16,2024]{1,0:T(8,128)(2,1)S(1)}, u32[]{:S(2)}, u32[]{:S(2)}) collective-permute-start(bf16[16,2024]{1,0:T(8,128)(2,1)S(1)} %constant_dynamic-update-slice_fusion), channel_id=1, source_target_pairs={{0,2},{1,3},{2,0},{3,1},{4,6},{5,7},{6,4},{7,5},{8,10},{9,11},{10,... | collective-permute-start | bytes 194312 | tf_op jit(solution)/shard_map/ppermute | solution.py:31
  13.7 8.3 %collective-permute-start.2 = (bf16[16,2024]{1,0:T(8,128)(2,1)S(1)}, bf16[16,2024]{1,0:T(8,128)(2,1)S(1)}, u32[]{:S(2)}, u32[]{:S(2)}) collective-permute-start(bf16[16,2024]{1,0:T(8,128)(2,1)S(1)} %constant_dynamic-update-slice_fusion), channel_id=1, source_target_pairs={{0,3},{1,2},{2,1},{3,0},{4,7},{5,6},{6,5},{7,4},{8,11},{9,10},{10,... | collective-permute-start | bytes 194312 | tf_op jit(solution)/shard_map/ppermute | solution.py:31
  13.7 8.4 %collective-permute-start.3 = (bf16[16,2024]{1,0:T(8,128)(2,1)S(1)}, bf16[16,2024]{1,0:T(8,128)(2,1)S(1)}, u32[]{:S(2)}, u32[]{:S(2)}) collective-permute-start(bf16[16,2024]{1,0:T(8,128)(2,1)S(1)} %constant_dynamic-update-slice_fusion), channel_id=1, source_target_pairs={{0,4},{1,5},{2,6},{3,7},{4,0},{5,1},{6,2},{7,3},{8,12},{9,13},{10,... | collective-permute-start | bytes 194312 | tf_op jit(solution)/shard_map/ppermute | solution.py:31
  16.4 7.5 %collective-permute-start.4 = (bf16[16,2024]{1,0:T(8,128)(2,1)S(1)}, bf16[16,2024]{1,0:T(8,128)(2,1)S(1)}, u32[]{:S(2)}, u32[]{:S(2)}) collective-permute-start(bf16[16,2024]{1,0:T(8,128)(2,1)S(1)} %constant_dynamic-update-slice_fusion), channel_id=1, source_target_pairs={{0,5},{1,4},{2,7},{3,6},{4,1},{5,0},{6,3},{7,2},{8,13},{9,12},{10,... | collective-permute-start | bytes 194312 | tf_op jit(solution)/shard_map/ppermute | solution.py:31
  19.4 5.4 %collective-permute-start.5 = (bf16[16,2024]{1,0:T(8,128)(2,1)S(1)}, bf16[16,2024]{1,0:T(8,128)(2,1)S(1)}, u32[]{:S(2)}, u32[]{:S(2)}) collective-permute-start(bf16[16,2024]{1,0:T(8,128)(2,1)S(1)} %constant_dynamic-update-slice_fusion), channel_id=1, source_target_pairs={{0,6},{1,7},{2,4},{3,5},{4,2},{5,3},{6,0},{7,1},{8,14},{9,15},{10,... | collective-permute-start | bytes 194312 | tf_op jit(solution)/shard_map/ppermute | solution.py:31
  21.9 6.8 %collective-permute-start.6 = (bf16[16,2024]{1,0:T(8,128)(2,1)S(1)}, bf16[16,2024]{1,0:T(8,128)(2,1)S(1)}, u32[]{:S(2)}, u32[]{:S(2)}) collective-permute-start(bf16[16,2024]{1,0:T(8,128)(2,1)S(1)} %constant_dynamic-update-slice_fusion), channel_id=1, source_target_pairs={{0,7},{1,6},{2,5},{3,4},{4,3},{5,2},{6,1},{7,0},{8,15},{9,14},{10,... | collective-permute-start | bytes 194312 | tf_op jit(solution)/shard_map/ppermute | solution.py:31
  35.4 9.6 %all-to-all-start = ((s32[8,128,1]{1,2,0:T(1,128)}), s32[8,128,1]{1,2,0:T(1,128)S(1)}, u32[]{:S(2)}, u32[]{:S(2)}) async-start(s32[8,128,1]{1,2,0:T(1,128)} %bitcast.15), calls=%async_computation | async-start | bytes 8192 | tf_op jit(solution)/shard_map/all_to_all | solution.py:59
  45.0 12.0 %all-to-all-start.1 = ((f32[8,128,128]{2,1,0:T(8,128)}), f32[8,128,128]{2,1,0:T(8,128)S(1)}, u32[]{:S(2)}, u32[]{:S(2)}) async-start(f32[8,128,128]{2,1,0:T(8,128)} %bitcast.17), calls=%async_computation.1 | async-start | bytes 1048576 | tf_op jit(solution)/shard_map/all_to_all | solution.py:60
  140.2 44.2 %copy-start.1 = (f32[128]{0:T(128)S(1)}, f32[128]{0:T(128)}, u32[]{:S(2)}) copy-start(f32[128]{0:T(128)} %param.10) | copy-start | bytes 1540
  177.8 14.0 %all-to-all-start.5 = ((f32[8,16,1000]{2,1,0:T(8,128)}), f32[8,16,1000]{2,1,0:T(8,128)S(1)}, u32[]{:S(2)}, u32[]{:S(2)}) async-start(f32[8,16,1000]{2,1,0:T(8,128)} %tile.8), calls=%async_computation.5 | async-start | bytes 1048576 | tf_op jit(solution)/shard_map/all_to_all | solution.py:18
  191.8 3.7 %copy-start = (pred[2048,1024]{1,0:T(32,128)(4,1)S(1)}, pred[2048,1024]{1,0:T(32,128)(4,1)}, u32[]{:S(2)}) copy-start(pred[2048,1024]{1,0:T(32,128)(4,1)} %iota_compare_fusion) | copy-start | bytes 6291460
Sparse Core Ops, SparseCore 0:
  30.3 57.8 all-gather.1

commit v4 on v3

--- a/solution.py
+++ b/solution.py
@@ -23,22 +23,11 @@
     return gather_back(gather_back(part, "blk"), "group")
 
 
-def exchange_gather(value, axis):
-    size = lax.axis_size(axis)
-    me = lax.axis_index(axis)
-    got = [value]
-    for d in range(1, size):
-        got.append(lax.ppermute(value, axis, [(k, k ^ d) for k in range(size)]))
-    stacked = jnp.stack(got)
-    order = jnp.arange(size, dtype=jnp.int32) ^ me
-    return stacked[order].reshape((-1,) + value.shape[1:])
-
-
 def body(centres, batch_x, grad, eigvec, eig_scale, sub_index):
     dims = batch_x.shape[1]
     centre_sq = jnp.sum(jnp.square(centres.astype(jnp.float32)), axis=1)
     joined = jnp.concatenate([batch_x, grad], axis=1)
-    joined = exchange_gather(joined, "group")
+    joined = gather_back(joined, "group")
     joined = lax.all_gather(joined, "blk", axis=0, tiled=True)
     piece_x = joined[:, :dims]
     piece_g = joined[:, dims:]

time: 216 us -> 211 us (0.977)
  blocking collectives: 36.5 us -> 54.3 us
  starting transfers between devices: 24.3 us -> 10.6 us
  waiting for transfers between devices: 53.4 us -> 46.6 us
  local copies, waits for them, and re-layouts: 29.4 us -> 26.4 us
    all_to_all x1 -> x2, blocking collectives: 8.69 us -> 26.5 us  [gather_back(): lax.all_to_all(jnp.tile(value, (size, 1)), axis, split_axis=0, concat_axi...]
    ppermute x7 -> x0, starting transfers between devices: 13.9 us -> none  [exchange_gather(): got.append(lax.ppermute(value, axis, [(k, k ^ d) for k in range(size)]))]
    ppermute x7 -> x0, waiting for transfers between devices: 6.65 us -> none  [exchange_gather(): got.append(lax.ppermute(value, axis, [(k, k ^ d) for k in range(size)]))]
  transfers between devices with their start and end apart: 11 -> 4, of which waited for: 7 -> 4; matrix products, arithmetic and copies ran while one was open for 7% -> 7% of each run, Pallas kernels for 0% -> 0%
where the time goes in v4:
time: 211 us; the launch traced here: 210 us
  blocking collectives  54.3 us (26%)
  matrix products  46.7 us (22%)
  waiting for transfers between devices  46.6 us (22%)
  local copies, waits for them, and re-layouts  26.4 us (13%)
  between operations  13.5 us (6%)
  other arithmetic  12.3 us (6%)
  starting transfers between devices  10.6 us (5%)
    all_gather x1, waiting for transfers between devices, body(): joined = lax.all_gather(joined, 'blk', axis=0, tiled=True)  30.6 us
    all_to_all x2, blocking collectives, scatter_sum(): got = lax.all_to_all(value, axis, split_axis=0, concat_axis=0, tiled=True)  27.8 us
    all_to_all x2, blocking collectives, gather_back(): lax.all_to_all(jnp.tile(value, (size, 1)), axis, split_axis=0, concat_axi...  26.5 us
    dot_general x1, matrix products, body(): jnp.dot(kernel_tile, piece_g, preferred_element_type=jnp.float32)  25.4 us
    dot_general x1, matrix products, body(): jnp.dot(jnp.concatenate([hits, hits], axis=1), jnp.concatenate([upper, lo...  13.1 us
    gather x1, local copies, waits for them, and re-layouts, body(): picked = kernel_grad[got_slots]  9.82 us
    dot_general x1, local copies, waits for them, and re-layouts, body(): jnp.dot(kernel_tile, piece_g, preferred_element_type=jnp.float32)  9.24 us
    all_to_all x1, waiting for transfers between devices, gather_back(): lax.all_to_all(jnp.tile(value, (size, 1)), axis, split_axis=0, concat_axi...  7.3 us
  transfers between devices with their start and end apart: 4, of which 4 were waited for; matrix products, arithmetic and copies ran while one was open for 7% of the time, Pallas kernels for 0%

profile of v4, /device:TPU:1, one launch (start us, length us, event | category | flops | bytes accessed | tf_op | source)
XLA Modules:
  0.0 210.4 jit_solution(10731175731696714076)
XLA Ops:
  6.5 0.8 pad_maximum_fusion
  7.4 17.8 %all_to_all.63 = bf16[8,16,2024]{2,1,0:T(8,128)(2,1)} all-to-all(bf16[8,16,2024]{2,1,0:T(8,128)(2,1)S(1)} %tile.8), channel_id=1, replica_groups=mesh['blk'=16,'group'=8] {'group'}, dimensions={0} | all-to-all | bytes 1036288 | tf_op jit(solution)/shard_map/all_to_all | solution.py:18
  25.2 0.0 all-gather.2.cloned.1.call-update
  25.2 0.7 add_select_fusion
  25.9 1.1 reduce-window.6
  27.1 0.2 slice_reduce_fusion
  27.3 0.1 fusion.29
  27.4 3.0 %scatter_custom_fusion = s32[1024]{0:T(1024)} fusion(s32[512]{0:T(512)S(1)} %compare_select_fusion.1, s32[512]{0:T(512)S(1)} %get-tuple-element.7, s32[]{:T(128)} %constant.51.clone.1), kind=kCustom, calls=%fused_computation.55 | custom fusion | bytes 4100 | tf_op jit(solution)/shard_map/scatter | solution.py:46
  30.4 3.4 %all-to-all-start.1 = ((s32[8,128,1]{1,2,0:T(1,128)}), s32[8,128,1]{1,2,0:T(1,128)S(1)}, u32[]{:S(2)}, u32[]{:S(2)}) async-start(s32[8,128,1]{1,2,0:T(1,128)} %bitcast.6), calls=%async_computation.1 | async-start | bytes 8192 | tf_op jit(solution)/shard_map/all_to_all | solution.py:48
  33.9 2.9 %scatter_custom_fusion.1 = f32[1024,128]{1,0:T(8,128)} fusion(s32[512]{0:T(512)S(1)} %compare_select_fusion.1, f32[512,128]{1,0:T(8,128)} %param.9, f32[]{:T(128)} %constant.48.clone.1), kind=kCustom, calls=%fused_computation.32 | custom fusion | bytes 524800 | tf_op jit(solution)/shard_map/scatter | solution.py:47
  36.8 3.5 %all-to-all-done.1 = s32[8,128,1]{1,2,0:T(1,128)S(1)} async-done(((s32[8,128,1]{1,2,0:T(1,128)}), s32[8,128,1]{1,2,0:T(1,128)S(1)}, u32[]{:S(2)}, u32[]{:S(2)}) %all-to-all-start.1) | async-done | bytes 4128 | tf_op jit(solution)/shard_map/all_to_all | solution.py:48
  40.3 3.7 %all-to-all-start.2 = ((f32[8,128,128]{2,1,0:T(8,128)}), f32[8,128,128]{2,1,0:T(8,128)S(1)}, u32[]{:S(2)}, u32[]{:S(2)}) async-start(f32[8,128,128]{2,1,0:T(8,128)} %bitcast.8), calls=%async_computation.2 | async-start | bytes 1048576 | tf_op jit(solution)/shard_map/all_to_all | solution.py:49
  43.9 3.2 %multiply_reduce_fusion.1 = f32[2048]{0:T(1024)S(1)} fusion(bf16[2048,1024]{1,0:T(8,128)(2,1)} %param.6), kind=kLoop, calls=%fused_computation.19 | loop fusion | flops 6289408 | bytes 4202496 | tf_op jit(solution)/shard_map/reduce_sum | solution.py:28
  47.1 5.2 %all-to-all-done.2 = f32[8,128,128]{2,1,0:T(8,128)S(1)} async-done(((f32[8,128,128]{2,1,0:T(8,128)}), f32[8,128,128]{2,1,0:T(8,128)S(1)}, u32[]{:S(2)}, u32[]{:S(2)}) %all-to-all-start.2) | async-done | bytes 524320 | tf_op jit(solution)/shard_map/all_to_all | solution.py:49
  52.3 0.2 copy.21
  52.5 30.6 %all-gather.2.cloned.1.call-done = bf16[2048,2024]{1,0:T(8,128)(2,1)} async-done(((bf16[128,2024]{1,0:T(8,128)(2,1)}), bf16[2048,2024]{1,0:T(8,128)(2,1)}) %all-gather.2.cloned.1.call-update) | async-done | bytes 8290320 | tf_op jit(solution)/shard_map/all_gather | solution.py:31
  83.1 3.1 %multiply_reduce_fusion = f32[2048]{0:T(1024)S(1)} fusion(bf16[2048,2024]{1,0:T(8,128)(2,1)} %all-gather.2.cloned.1.call-done), kind=kLoop, calls=%fused_computation.17 | loop fusion | flops 6289408 | bytes 4202496 | tf_op jit(solution)/shard_map/reduce_sum | solution.py:34
  86.2 25.4 %fusion.8 = f32[2048,1000]{0,1:T(8,128)} fusion(bf16[2048,1024]{1,0:T(8,128)(2,1)} %param.6, f32[2048]{0:T(1024)S(1)} %multiply_reduce_fusion, f32[2048]{0:T(1024)S(1)} %multiply_reduce_fusion.1, bf16[2048,2024]{1,0:T(8,128)(2,1)} %all-gather.2.cloned.1.call-done), kind=kOutput, calls=%fused_computation.12 | convolution fusion | flops 17003708416 | bytes 20692992 | tf_op jit(solution)/shard_map/dot_general | solution.py:38
  111.6 9.2 %copy.18 = f32[2048,1000]{1,0:T(8,128)} copy(f32[2048,1000]{0,1:T(8,128)} %fusion.8) | data formatting | bytes 16384000 | tf_op jit(solution)/shard_map/dot_general | solution.py:38
  120.8 9.8 %gather_fusion = f32[1024,1000]{1,0:T(8,128)} fusion(f32[2048,1000]{1,0:T(8,128)} %copy.18, s32[1024]{0:T(1024)S(1)} %broadcast_clamp_fusion), kind=kCustom, calls=%fused_computation | custom fusion | bytes 8196096 | tf_op jit(solution)/shard_map/gather | solution.py:50
  130.6 4.6 %fusion.14 = f32[8,16,1000]{2,1,0:T(8,128)S(1)} fusion(f32[8,16,1024]{2,1,0:T(8,128)S(1)} %bitcast.46, f32[1024,1000]{1,0:T(8,128)} %gather_fusion), kind=kOutput, calls=%fused_computation.23 | convolution fusion | flops 1572864000 | bytes 5132288 | tf_op jit(solution)/shard_map/sq,sk->qk/dot_general | solution.py:51
  135.2 0.0 copy-start.1
  135.2 16.1 %all_to_all.64 = f32[8,16,1000]{2,1,0:T(8,128)S(1)} all-to-all(f32[8,16,1000]{2,1,0:T(8,128)S(1)} %fusion.14), channel_id=1, replica_groups=mesh['blk'=16,'group'=8] {'group'}, dimensions={0} | all-to-all | bytes 1024000 | tf_op jit(solution)/shard_map/all_to_all | solution.py:12
  151.4 11.7 %all_to_all.65 = f32[16,1,1000]{2,1,0:T(1,128)S(1)} all-to-all(f32[16,1,1000]{2,1,0:T(1,128)S(1)} %all_to_all.51), channel_id=1, replica_groups=mesh['blk'=16,'group'=8] {'blk'}, dimensions={0} | all-to-all | bytes 128000 | tf_op jit(solution)/shard_map/all_to_all | solution.py:12
  163.1 0.1 reduce_sum.49
  163.2 8.7 %all_to_all.66 = f32[16,1,1000]{2,1,0:T(1,128)S(1)} all-to-all(f32[16,1,1000]{2,1,0:T(1,128)S(1)} %tile.9), channel_id=1, replica_groups=mesh['blk'=16,'group'=8] {'blk'}, dimensions={0} | all-to-all | bytes 128000 | tf_op jit(solution)/shard_map/all_to_all | solution.py:18
  171.9 0.9 tile.11
  172.8 3.5 %all-to-all-start.6 = ((f32[8,16,1000]{2,1,0:T(8,128)}), f32[8,16,1000]{2,1,0:T(8,128)S(1)}, u32[]{:S(2)}, u32[]{:S(2)}) async-start(f32[8,16,1000]{2,1,0:T(8,128)} %tile.11), calls=%async_computation.6 | async-start | bytes 1048576 | tf_op jit(solution)/shard_map/all_to_all | solution.py:18
  176.2 3.1 %iota_compare_fusion = pred[2048,1024]{1,0:T(32,128)(4,1)} fusion(s32[1024]{0:T(1024)S(1)} %bitcast.50), kind=kLoop, calls=%fused_computation.13 | loop fusion | flops 2097152 | bytes 2101248 | tf_op jit(solution)/shard_map/eq | solution.py:57
  179.4 7.3 %all-to-all-done.6 = f32[8,16,1000]{2,1,0:T(8,128)S(1)} async-done(((f32[8,16,1000]{2,1,0:T(8,128)}), f32[8,16,1000]{2,1,0:T(8,128)S(1)}, u32[]{:S(2)}, u32[]{:S(2)}) %all-to-all-start.6) | async-done | bytes 512032 | tf_op jit(solution)/shard_map/all_to_all | solution.py:18
  186.7 3.7 %reduce-precision_convert_fusion = (bf16[1024,1000]{0,1:T(8,128)(2,1)S(1)}, bf16[1024,1000]{0,1:T(8,128)(2,1)S(1)}) fusion(f32[1024,128]{1,0:T(8,128)S(1)} %bitcast.47, f32[128,1000]{1,0:T(8,128)S(1)} %bitcast.45), kind=kOutput, calls=%fused_computation.21 | convolution fusion | flops 1576960000 | bytes 5132288 | tf_op jit(solution)/shard_map/dot_general | solution.py:53
  190.5 13.1 %fusion.18 = f32[2048,1000]{0,1:T(8,128)} fusion(f32[2048,1000]{0,1:T(8,128)} %fusion.8, pred[2048,1024]{1,0:T(32,128)(4,1)S(1)} %copy-done, bf16[1024,1000]{0,1:T(8,128)(2,1)S(1)} %get-tuple-element.6, bf16[1024,1000]{0,1:T(8,128)(2,1)S(1)} %get-tuple-element.5), kind=kOutput, calls=%fused_computation.27 | convolution fusion | flops 8403042304 | bytes 22577152 | tf_op jit(solution)/shard_map/dot_general | solution.py:58
  (16 shorter events, 0.3 us)
Async XLA Ops:
  6.5 76.6 %all-gather.2.cloned.1.call-start = ((), (), s32[]{:S(2)}) async-start(), calls=%async_computation.7 | async-start | bytes 8912896 | tf_op jit(solution)/shard_map/all_gather | solution.py:31
  30.4 9.8 %all-to-all-start.1 = ((s32[8,128,1]{1,2,0:T(1,128)}), s32[8,128,1]{1,2,0:T(1,128)S(1)}, u32[]{:S(2)}, u32[]{:S(2)}) async-start(s32[8,128,1]{1,2,0:T(1,128)} %bitcast.6), calls=%async_computation.1 | async-start | bytes 8192 | tf_op jit(solution)/shard_map/all_to_all | solution.py:48
  40.3 12.1 %all-to-all-start.2 = ((f32[8,128,128]{2,1,0:T(8,128)}), f32[8,128,128]{2,1,0:T(8,128)S(1)}, u32[]{:S(2)}, u32[]{:S(2)}) async-start(f32[8,128,128]{2,1,0:T(8,128)} %bitcast.8), calls=%async_computation.2 | async-start | bytes 1048576 | tf_op jit(solution)/shard_map/all_to_all | solution.py:49
  135.2 44.2 %copy-start.1 = (f32[128]{0:T(128)S(1)}, f32[128]{0:T(128)}, u32[]{:S(2)}) copy-start(f32[128]{0:T(128)} %param.10) | copy-start | bytes 1540
  172.8 14.0 %all-to-all-start.6 = ((f32[8,16,1000]{2,1,0:T(8,128)}), f32[8,16,1000]{2,1,0:T(8,128)S(1)}, u32[]{:S(2)}, u32[]{:S(2)}) async-start(f32[8,16,1000]{2,1,0:T(8,128)} %tile.11), calls=%async_computation.6 | async-start | bytes 1048576 | tf_op jit(solution)/shard_map/all_to_all | solution.py:18
  186.7 3.7 %copy-start = (pred[2048,1024]{1,0:T(32,128)(4,1)S(1)}, pred[2048,1024]{1,0:T(32,128)(4,1)}, u32[]{:S(2)}) copy-start(pred[2048,1024]{1,0:T(32,128)(4,1)} %iota_compare_fusion) | copy-start | bytes 6291460
Sparse Core Ops, SparseCore 0:
  25.3 57.7 all-gather.1
